TPU v7x, 512 devices: a whole 4x4x16 slice. The times are simulated.
512 devices in a mesh: fit: 32 (over z, core), orb: 16 (over x, y).
Axes of the slice: x: 4, y: 4, z: 16, core: 2. Of those that a mesh axis runs over, the one named last changes fastest.
Arguments:
- half_ints: bfloat16 [16, 256, 768, 256], P('orb', None, 'fit'), may hold values from -6 to 6
- osv_coef: bfloat16 [16, 256, 256, 64], P('orb', 'fit'), may hold values from -0.09375 to 0.09375
- fit_blocks: int32 [16, 256, 6], P('orb', 'fit'), may hold values from 0 to 468, as said below
- partner_list: int32 [32, 16, 24], P('fit'), may hold values from 0 to 127, as said below
Outputs:
- pair_ints: bfloat16 [16, 256, 24, 4096], P('orb', 'fit')
Inputs may be any that keep to these rules, and one draw needn't show every extreme that they name: `fit_blocks`: the 6 block numbers of one orbital are distinct. `partner_list`: entry h * 8 + k names orbital k of the same column in group h. The 24 entries of one list are distinct. Of one list, at most 3 entries name orbitals of any one group, and in every list some group is named exactly 3 times.
All inputs are finite; a program needn't handle non-finite values.
Results may differ from a plain program's by a relative error of at most 0.0055.
Values may be sent and summed in bfloat16 or wider, within the bound.
No kernel may reach another device: no remote copies, remote signals or barrier semaphores. Data moves between devices by JAX's collectives and lax.ppermute only.
A program may use at most 64 MiB of HBM per device.

v0:
```python
import jax
import jax.numpy as jnp
from jax import lax
from jax.sharding import PartitionSpec as P

BLK = 128
FBLK = 6


def per_device(half_ints, osv_coef, fit_blocks, partner_list):
    local_rows = half_ints[0]
    own_ints = lax.all_to_all(local_rows, "fit", split_axis=0, concat_axis=1, tiled=True)
    osv_local = osv_coef[0]
    projected = jnp.einsum(
        "kfa,kao->kof", own_ints, osv_local, preferred_element_type=jnp.float32
    ).astype(jnp.bfloat16)
    own_blocks = fit_blocks[0]
    column_lists = partner_list[0]
    nosv_count = projected.shape[1]
    npart_count = column_lists.shape[1]
    my_group = lax.axis_index("orb")
    wanted = lax.dynamic_index_in_dim(column_lists, my_group, 0, keepdims=False)
    piece_rows = lax.all_gather(projected, "orb", axis=0, tiled=True)
    piece_blocks = lax.all_gather(own_blocks, "orb", axis=0, tiled=True)
    piece_len = piece_rows.shape[0]
    matches = wanted[:, None] == jnp.arange(piece_len, dtype=jnp.int32)[None, :]
    buffer = jnp.einsum(
        "nr,rxf->nxf", matches.astype(jnp.bfloat16), piece_rows, preferred_element_type=jnp.float32
    ).astype(jnp.bfloat16)
    blocks = jnp.sum(jnp.where(matches[:, :, None], piece_blocks[None, :, :], 0), axis=1).astype(
        jnp.int32
    )
    partner_pieces = buffer.reshape(npart_count, nosv_count, FBLK, BLK)

    def pair_block(operand):
        own_rows, own_ids = operand
        matching = (own_ids[None, :, None] == blocks[:, None, :]).astype(jnp.bfloat16)
        aligned = jnp.einsum(
            "nbc,nxcp->nxbp", matching, partner_pieces, preferred_element_type=jnp.float32
        ).astype(jnp.bfloat16)
        pair_vals = jnp.einsum(
            "abp,nxbp->nax",
            own_rows.reshape(nosv_count, FBLK, BLK),
            aligned,
            preferred_element_type=jnp.float32,
        )
        return pair_vals.astype(jnp.bfloat16).reshape(npart_count, nosv_count * nosv_count)

    result = lax.map(pair_block, (projected, own_blocks))
    return result[None]


def solution(mesh):
    return jax.shard_map(
        per_device,
        mesh=mesh,
        in_specs=(
            P("orb", None, "fit", None),
            P("orb", "fit", None, None),
            P("orb", "fit", None),
            P("fit", None, None),
        ),
        out_specs=P("orb", "fit", None, None),
        check_vma=False,
    )
```

profile of v0, /device:TPU:1, one launch (start us, length us, event | category | flops | bytes accessed | tf_op | source)
XLA Modules:
  0.0 406.4 jit_solution(8026830469797910473)
XLA Ops:
  6.5 162.5 %all_to_all.18 = bf16[256,24,256]{2,1,0:T(8,128)(2,1)S(1)} all-to-all(bf16[256,24,256]{2,1,0:T(8,128)(2,1)} %bitcast.55), channel_id=1, replica_groups=mesh['fit'=32,'orb'=16] {'fit'}, dimensions={0} | all-to-all | bytes 6291456 | tf_op jit(solution)/shard_map/all_to_all | solution.py:12
  169.2 2.0 convolution_convert_fusion
  171.4 19.8 %all-gather = s32[1,128,6]{2,0,1:T(1,128)S(1)} all-gather(s32[1,8,6]{2,0,1:T(1,128)S(1)} %copy.31), channel_id=2, replica_groups=mesh['fit'=32,'orb'=16] {'orb'}, dimensions={1}, use_global_device_ids=true | all-gather | bytes 3264 | tf_op jit(solution)/shard_map/all_gather | solution.py:24
  192.4 75.6 %all-gather.3.cloned.1.call-done = bf16[128,64,768]{2,1,0:T(8,128)(2,1)} async-done(((bf16[8,64,768]{2,1,0:T(8,128)(2,1)}), bf16[128,64,768]{2,1,0:T(8,128)(2,1)}) %all-gather.3.cloned.1.call-update) | async-done | bytes 12582928 | tf_op jit(solution)/shard_map/all_gather | solution.py:23
  268.0 18.0 %fusion.20 = bf16[24,64,768]{2,0,1:T(8,128)(2,1)S(1)} fusion(bf16[128,64,768]{2,1,0:T(8,128)(2,1)} %all-gather.3.cloned.1.call-done, s32[24]{0:T(128)S(1)} %dynamic-slice_bitcast_fusion), kind=kOutput, calls=%fused_computation.18 | convolution fusion | flops 303172608 | bytes 14942304 | tf_op jit(solution)/shard_map/nr,rxf->nxf/dot_general | solution.py:27
  286.0 1.9 copy.35
  287.9 4.8 %reshape.40 = bf16[24,64,6,128]{3,2,1,0:T(8,128)(2,1)S(1)} reshape(bf16[24,64,768]{2,1,0:T(8,128)(2,1)} %copy.35) | data formatting | bytes 4718592 | tf_op jit(solution)/shard_map/reshape | solution.py:33
  292.8 106.8 %while.10 = (s32[]{:T(128)}, bf16[8,24,4096]{2,1,0:T(8,128)(2,1)}, s32[8,6]{1,0:T(8,128)S(1)}, s32[24,6]{1,0:T(8,128)S(1)}, bf16[24,64,6,128]{3,2,1,0:T(8,128)(2,1)S(1)}, /*index=5*/bf16[8,64,768]{2,1,0:T(8,128)(2,1)}, s32[]{:T(128)}) while((s32[]{:T(128)}, bf16[8,24,4096]{2,1,0:T(8,128)(2,1)}, s32[8,6]{1,0:T(8,128)S(1)}, ...), condition=%wide.region_2.3_spmd, body=%wide.region_1.2_spmd.sunk | while | flops 166429536 | bytes 8946909 | solution.py:49
  292.8 2.7 convert_bitcast_fusion.2
  297.1 3.4 fusion.38
  302.5 2.0 broadcast_in_dim.45
  306.1 2.7 convert_bitcast_fusion.2
  310.5 3.4 fusion.38
  315.8 2.0 broadcast_in_dim.45
  319.5 2.7 convert_bitcast_fusion.2
  323.8 3.4 fusion.38
  329.2 2.0 broadcast_in_dim.45
  332.8 2.7 convert_bitcast_fusion.2
  337.2 3.4 fusion.38
  342.5 2.0 broadcast_in_dim.45
  346.2 2.7 convert_bitcast_fusion.2
  350.5 3.4 fusion.38
  355.9 2.0 broadcast_in_dim.45
  359.5 2.7 convert_bitcast_fusion.2
  363.9 3.4 fusion.38
  369.2 2.0 broadcast_in_dim.45
  372.9 2.7 convert_bitcast_fusion.2
  377.2 3.4 fusion.38
  382.6 2.0 broadcast_in_dim.45
  386.2 2.7 convert_bitcast_fusion.2
  390.6 3.4 fusion.38
  395.9 2.0 broadcast_in_dim.45
  (55 shorter events, 43.3 us)
Async XLA Ops:
  6.5 162.7 %copy-start = (bf16[1,8,256,64]{2,3,1,0:T(8,128)(2,1)S(1)}, bf16[1,8,256,64]{2,3,1,0:T(8,128)(2,1)}, u32[]{:S(2)}) copy-start(bf16[1,8,256,64]{2,3,1,0:T(8,128)(2,1)} %param.7) | copy-start | bytes 786436
  6.5 261.4 %all-gather.3.cloned.1.call-start = ((), (), s32[]{:S(2)}) async-start(), calls=%async_computation.1 | async-start | bytes 13369344 | tf_op jit(solution)/shard_map/all_gather | solution.py:23
  169.2 2.1 copy-start.1
Sparse Core Ops, SparseCore 0:
  171.4 96.5 all-gather.2
where the time goes:
time: 408 us; the launch traced here: 406 us
  blocking collectives  182 us (45%)
  waiting for transfers between devices  75.6 us (19%)
  matrix products  68.8 us (17%)
  local copies, waits for them, and re-layouts  66 us (16%)
  between operations  13.5 us (3%)
    all_to_all x1, blocking collectives, per_device(): lax.all_to_all(local_rows, 'fit', split_axis=0, concat_axis=1, tiled=True)  162 us
    all_gather x1, waiting for transfers between devices, per_device(): piece_rows = lax.all_gather(projected, 'orb', axis=0, tiled=True)  75.6 us
    dot_general x8, matrix products, pair_block(): jnp.einsum('abp,nxbp->nax', own_rows.reshape(nosv_count, FBLK, BLK), alig...  27.3 us
    dot_general x8, matrix products, pair_block(): jnp.einsum('nbc,nxcp->nxbp', matching, partner_pieces, preferred_element_...  21.5 us
    all_gather x1, blocking collectives, per_device(): piece_blocks = lax.all_gather(own_blocks, 'orb', axis=0, tiled=True)  19.8 us
    dot_general x1, matrix products, per_device(): jnp.einsum('nr,rxf->nxf', matches.astype(jnp.bfloat16), piece_rows, prefe...  18 us
    broadcast_in_dim x8, local copies, waits for them, and re-layouts, per_device(): result = lax.map(pair_block, (projected, own_blocks))  16.3 us
    convert_element_type x8, local copies, waits for them, and re-layouts, pair_block(): pair_vals.astype(jnp.bfloat16).reshape(npart_count, nosv_count * nosv_count)  15.4 us
  transfers between devices with their start and end apart: 1, of which 1 were waited for; matrix products, arithmetic and copies ran while one was open for 0% of the time, Pallas kernels for 0%

commit v1 on v0

--- a/solution.py
+++ b/solution.py
@@ -9,7 +9,15 @@
 
 def per_device(half_ints, osv_coef, fit_blocks, partner_list):
     local_rows = half_ints[0]
-    own_ints = lax.all_to_all(local_rows, "fit", split_axis=0, concat_axis=1, tiled=True)
+    own_ints = jnp.concatenate(
+        lax.all_to_all(
+            jnp.stack(jnp.split(local_rows, lax.axis_size("fit"), axis=0), axis=0),
+            axis_name="fit",
+            split_axis=0,
+            concat_axis=0,
+        ),
+        axis=1,
+    )
     osv_local = osv_coef[0]
     projected = jnp.einsum(
         "kfa,kao->kof", own_ints, osv_local, preferred_element_type=jnp.float32

time: 408 us -> 437 us (1.071)
  local copies, waits for them, and re-layouts: 66 us -> 94.8 us
    unnamed x6 -> x37, local copies, waits for them, and re-layouts: 0.17 us -> 28.1 us
where the time goes in v1:
time: 437 us; the launch traced here: 435 us
  blocking collectives  182 us (42%)
  local copies, waits for them, and re-layouts  94.8 us (22%)
  waiting for transfers between devices  75.6 us (17%)
  matrix products  68.8 us (16%)
  between operations  13.5 us (3%)
    all_to_all x1, blocking collectives, per_device(): lax.all_to_all(jnp.stack(jnp.split(local_rows, lax.axis_size('fit'), axis...  162 us
    all_gather x1, waiting for transfers between devices, per_device(): piece_rows = lax.all_gather(projected, 'orb', axis=0, tiled=True)  75.6 us
    unnamed x37, local copies, waits for them, and re-layouts  28.1 us
    dot_general x8, matrix products, pair_block(): jnp.einsum('abp,nxbp->nax', own_rows.reshape(nosv_count, FBLK, BLK), alig...  27.3 us
    dot_general x8, matrix products, pair_block(): jnp.einsum('nbc,nxcp->nxbp', matching, partner_pieces, preferred_element_...  21.5 us
    all_gather x1, blocking collectives, per_device(): piece_blocks = lax.all_gather(own_blocks, 'orb', axis=0, tiled=True)  19.8 us
    dot_general x1, matrix products, per_device(): jnp.einsum('nr,rxf->nxf', matches.astype(jnp.bfloat16), piece_rows, prefe...  18 us
    broadcast_in_dim x8, local copies, waits for them, and re-layouts, per_device(): result = lax.map(pair_block, (projected, own_blocks))  16.3 us
  transfers between devices with their start and end apart: 1, of which 1 were waited for; matrix products, arithmetic and copies ran while one was open for 0% of the time, Pallas kernels for 0%

profile of v1, /device:TPU:1, one launch (start us, length us, event | category | flops | bytes accessed | tf_op | source)
XLA Modules:
  0.0 434.9 jit_solution(3600475967406332993)
XLA Ops:
  35.4 162.1 %all_to_all.5 = bf16[32,8,24,256]{3,2,1,0:T(8,128)(2,1)S(1)} all-to-all(bf16[32,8,24,256]{3,2,1,0:T(8,128)(2,1)S(1)} %slice_dynamic-update-slice_fusion), channel_id=1, replica_groups=mesh['fit'=32,'orb'=16] {'fit'}, dimensions={0} | all-to-all | bytes 6291456 | tf_op jit(solution)/shard_map/all_to_all | solution.py:13
  197.7 2.0 fusion.23
  199.9 19.8 %all-gather = s32[1,128,6]{2,0,1:T(1,128)S(1)} all-gather(s32[1,8,6]{2,0,1:T(1,128)S(1)} %copy.31), channel_id=2, replica_groups=mesh['fit'=32,'orb'=16] {'orb'}, dimensions={1}, use_global_device_ids=true | all-gather | bytes 3264 | tf_op jit(solution)/shard_map/all_gather | solution.py:32
  220.9 75.6 %all-gather.3.cloned.1.call-done = bf16[128,64,768]{2,1,0:T(8,128)(2,1)} async-done(((bf16[8,64,768]{2,1,0:T(8,128)(2,1)}), bf16[128,64,768]{2,1,0:T(8,128)(2,1)}) %all-gather.3.cloned.1.call-update) | async-done | bytes 12582928 | tf_op jit(solution)/shard_map/all_gather | solution.py:31
  296.5 18.0 %fusion.20 = bf16[24,64,768]{2,0,1:T(8,128)(2,1)S(1)} fusion(bf16[128,64,768]{2,1,0:T(8,128)(2,1)} %all-gather.3.cloned.1.call-done, s32[24]{0:T(128)S(1)} %dynamic-slice_bitcast_fusion), kind=kOutput, calls=%fused_computation.18 | convolution fusion | flops 303172608 | bytes 14942304 | tf_op jit(solution)/shard_map/nr,rxf->nxf/dot_general | solution.py:35
  314.5 1.9 copy.35
  316.4 4.8 %reshape.112 = bf16[24,64,6,128]{3,2,1,0:T(8,128)(2,1)S(1)} reshape(bf16[24,64,768]{2,1,0:T(8,128)(2,1)} %copy.35) | data formatting | bytes 4718592 | tf_op jit(solution)/shard_map/reshape | solution.py:41
  321.2 106.8 %while.10 = (s32[]{:T(128)}, bf16[8,24,4096]{2,1,0:T(8,128)(2,1)}, s32[8,6]{1,0:T(8,128)S(1)}, s32[24,6]{1,0:T(8,128)S(1)}, bf16[24,64,6,128]{3,2,1,0:T(8,128)(2,1)S(1)}, /*index=5*/bf16[8,64,768]{2,1,0:T(8,128)(2,1)}, s32[]{:T(128)}) while((s32[]{:T(128)}, bf16[8,24,4096]{2,1,0:T(8,128)(2,1)}, s32[8,6]{1,0:T(8,128)S(1)}, ...), condition=%wide.region_2.3_spmd, body=%wide.region_1.2_spmd.sunk | while | flops 166429536 | bytes 8946909 | solution.py:57
  321.3 2.7 convert_bitcast_fusion.2
  325.6 3.4 fusion.39
  331.0 2.0 broadcast_in_dim.45
  334.6 2.7 convert_bitcast_fusion.2
  339.0 3.4 fusion.39
  344.3 2.0 broadcast_in_dim.45
  348.0 2.7 convert_bitcast_fusion.2
  352.3 3.4 fusion.39
  357.7 2.0 broadcast_in_dim.45
  361.3 2.7 convert_bitcast_fusion.2
  365.7 3.4 fusion.39
  371.0 2.0 broadcast_in_dim.45
  374.7 2.7 convert_bitcast_fusion.2
  379.0 3.4 fusion.39
  384.4 2.0 broadcast_in_dim.45
  388.0 2.7 convert_bitcast_fusion.2
  392.4 3.4 fusion.39
  397.7 2.0 broadcast_in_dim.45
  401.4 2.7 convert_bitcast_fusion.2
  405.7 3.4 fusion.39
  411.1 2.0 broadcast_in_dim.45
  414.7 2.7 convert_bitcast_fusion.2
  419.1 3.4 fusion.39
  424.4 2.0 broadcast_in_dim.45
  (87 shorter events, 72.1 us)
Async XLA Ops:
  6.5 191.2 %copy-start = (bf16[1,8,256,64]{2,3,1,0:T(8,128)(2,1)S(1)}, bf16[1,8,256,64]{2,3,1,0:T(8,128)(2,1)}, u32[]{:S(2)}) copy-start(bf16[1,8,256,64]{2,3,1,0:T(8,128)(2,1)} %param.7) | copy-start | bytes 786436
  6.5 289.9 %all-gather.3.cloned.1.call-start = ((), (), s32[]{:S(2)}) async-start(), calls=%async_computation.1 | async-start | bytes 13369344 | tf_op jit(solution)/shard_map/all_gather | solution.py:31
  197.7 2.1 copy-start.1
Sparse Core Ops, SparseCore 0:
  199.9 96.5 all-gather.2
